TPU v7x, 256 devices: a whole 4x4x8 slice. The times are simulated.
256 devices in a mesh: dp: 4 (over x), expert: 64 (over y, z, core).
Axes of the slice: x: 4, y: 4, z: 8, core: 2. Of those that a mesh axis runs over, the one named last changes fastest.
Arguments:
- features: bfloat16 [65536, 512], P(('dp', 'expert')), may hold values from -6 to 6
- slots: int32 [65536], P(('dp', 'expert')), may hold values from 0 to 31
- routes: int32 [65536, 2], P(('dp', 'expert')), may hold values from 0 to 63, all different within a row; in each aligned block of 256 rows (0 to 255, 256 to 511, ...) at most 16 rows name the same one
- cotangent: bfloat16 [65536, 512], P(('dp', 'expert')), may hold values from -1.5 to 1.5
- pos_table: bfloat16 [32, 64], replicated, may hold values from -6 to 6
- tower_in: bfloat16 [64, 256], replicated, may hold values from -0.75 to 0.75
- tower_out: bfloat16 [256, 512], replicated, may hold values from -0.375 to 0.375
- router: bfloat16 [512, 64], replicated, may hold values from -0.5 to 0.5
- w_up: bfloat16 [64, 512, 2048], P('expert'), may hold values from -0.25 to 0.25
- w_down: bfloat16 [64, 2048, 512], P('expert'), may hold values from -0.125 to 0.125
Outputs:
- layer_out: bfloat16 [65536, 512], P(('dp', 'expert'))
- grad_in: bfloat16 [65536, 512], P(('dp', 'expert'))
- grad_up: bfloat16 [64, 512, 2048], P('expert')
- grad_down: bfloat16 [64, 2048, 512], P('expert')
Inputs may be any that keep to these rules, and one draw needn't show every extreme that they name: `routes`: within the rows of one device no expert is named by more than 16 rows; in some devices' rows one expert is named by exactly 16.
All inputs are finite; a program needn't handle non-finite values.
Results may differ from a plain program's by a relative error of at most 0.013.
Values may be sent and summed in bfloat16 or wider, within the bound.
No kernel may reach another device: no remote copies, remote signals or barrier semaphores. Data moves between devices by JAX's collectives and lax.ppermute only.
A program may use at most 128 MiB of HBM per device.

v0:
```python
import jax
import jax.numpy as jnp
from jax import lax
from jax.sharding import PartitionSpec as P

TOP = 2
coef_a = 0.7978845608028654
coef_b = 0.044715


def gelu_pair(pre_act):
    inner = coef_a * (pre_act + coef_b * pre_act * pre_act * pre_act)
    tanh_val = jnp.tanh(inner)
    activated = 0.5 * pre_act * (1.0 + tanh_val)
    gelu_slope = 0.5 * (1.0 + tanh_val) + 0.5 * pre_act * (1.0 - tanh_val * tanh_val) * coef_a * (
        1.0 + 3.0 * coef_b * pre_act * pre_act
    )
    return (activated, gelu_slope)


def contract_rows(left, right):
    return lax.dot_general(
        left, right, (((0,), (0,)), ((), ())), preferred_element_type=jnp.float32
    )


def contract_cols(left, right):
    return lax.dot_general(
        left, right, (((1,), (1,)), ((), ())), preferred_element_type=jnp.float32
    )


def expert_forward(flat_in, w_up_one, w_down_one):
    pre_act = jnp.dot(flat_in, w_up_one, preferred_element_type=jnp.float32)
    activated, gelu_slope = gelu_pair(pre_act)
    hidden = activated.astype(jnp.bfloat16)
    outputs = jnp.dot(hidden, w_down_one, preferred_element_type=jnp.float32).astype(jnp.bfloat16)
    return (hidden, gelu_slope, outputs)


def expert_backward(flat_in, flat_cot, hidden, gelu_slope, w_up_one, w_down_one):
    grad_down_part = contract_rows(hidden, flat_cot)
    d_hidden = contract_cols(flat_cot, w_down_one)
    d_pre = (d_hidden * gelu_slope).astype(jnp.bfloat16)
    d_inputs = contract_cols(d_pre, w_up_one).astype(jnp.bfloat16)
    grad_up_part = contract_rows(flat_in, d_pre)
    sum_up, sum_down = (
        lax.psum(grad_up_part.astype(jnp.bfloat16), "dp").astype(jnp.float32),
        lax.psum(grad_down_part.astype(jnp.bfloat16), "dp").astype(jnp.float32),
    )
    return (d_inputs, sum_up, sum_down)


def per_device(
    features, slots, routes, cotangent, pos_table, tower_in, tower_out, router, w_up, w_down
):
    tok_rows = features.shape[0]
    feature_width = features.shape[1]
    n_experts = router.shape[1]
    capacity = 2 * TOP * tok_rows // n_experts
    pos_hidden = jax.nn.relu(jnp.dot(pos_table, tower_in, preferred_element_type=jnp.float32))
    pos_rows = jnp.dot(pos_hidden, tower_out.astype(jnp.float32), precision=lax.Precision.HIGHEST)
    slot_hot = (slots[:, None] == jnp.arange(pos_table.shape[0], dtype=jnp.int32)[None, :]).astype(
        jnp.float32
    )
    pos_feats = jnp.dot(slot_hot, pos_rows, precision=lax.Precision.HIGHEST)
    mixed_in = (features.astype(jnp.float32) + pos_feats).astype(jnp.bfloat16)
    logits = jnp.dot(mixed_in, router, preferred_element_type=jnp.float32)
    expert_ids = jnp.arange(n_experts, dtype=jnp.int32)
    route_hot = routes[:, :, None] == expert_ids[None, None, :]
    chosen = jnp.sum(jnp.where(route_hot, logits[:, None, :], 0.0), axis=2)
    squashed = 1.0 / (1.0 + jnp.exp(-chosen))
    gate_total = jnp.sum(squashed, axis=1, keepdims=True)
    gates = squashed / gate_total
    cot_wide = cotangent.astype(jnp.float32)
    slot_cot = (gates[:, :, None] * cot_wide[:, None, :]).astype(jnp.bfloat16)
    flat_routes = routes.reshape(-1)
    flat_hot = route_hot.reshape(-1, n_experts).astype(jnp.int32)
    before = jnp.cumsum(flat_hot, axis=0, dtype=jnp.int32) - flat_hot
    slot_rank = jnp.sum(before * flat_hot, axis=1, dtype=jnp.int32)
    slot_place = flat_routes * capacity + slot_rank
    buffer_shape = (n_experts, capacity, feature_width)
    send_in = (
        jnp.zeros((n_experts * capacity, feature_width), jnp.bfloat16)
        .at[slot_place]
        .set(jnp.repeat(mixed_in, TOP, axis=0))
        .reshape(buffer_shape)
    )
    send_cot = (
        jnp.zeros((n_experts * capacity, feature_width), jnp.bfloat16)
        .at[slot_place]
        .set(slot_cot.reshape(-1, feature_width))
        .reshape(buffer_shape)
    )
    w_up_one = w_up[0]
    w_down_one = w_down[0]
    recv_in = lax.all_to_all(send_in, "expert", split_axis=0, concat_axis=0, tiled=True)
    flat_in = recv_in.reshape(-1, feature_width)
    hidden, gelu_slope, outputs = expert_forward(flat_in, w_up_one, w_down_one)
    back_out = lax.all_to_all(
        outputs.reshape(buffer_shape), "expert", split_axis=0, concat_axis=0, tiled=True
    )
    recv_cot = lax.all_to_all(send_cot, "expert", split_axis=0, concat_axis=0, tiled=True)
    flat_cot = recv_cot.reshape(-1, feature_width)
    d_inputs, sum_up, sum_down = expert_backward(
        flat_in, flat_cot, hidden, gelu_slope, w_up_one, w_down_one
    )
    back_grad = lax.all_to_all(
        d_inputs.reshape(buffer_shape), "expert", split_axis=0, concat_axis=0, tiled=True
    )
    expert_out = back_out.reshape(-1, feature_width)[slot_place].reshape(
        tok_rows, TOP, feature_width
    )
    slot_grad = back_grad.reshape(-1, feature_width)[slot_place].reshape(
        tok_rows, TOP, feature_width
    )
    expert_wide = expert_out.astype(jnp.float32)
    layer_out = (
        mixed_in.astype(jnp.float32) + jnp.sum(gates[:, :, None] * expert_wide, axis=1)
    ).astype(jnp.bfloat16)
    d_gates = jnp.sum(expert_wide * cot_wide[:, None, :], axis=2)
    mean_term = jnp.sum(gates * d_gates, axis=1, keepdims=True)
    d_chosen = (d_gates - mean_term) / gate_total * squashed * (1.0 - squashed)
    d_logits = jnp.sum(jnp.where(route_hot, d_chosen[:, :, None], 0.0), axis=1)
    d_router = lax.dot_general(
        d_logits,
        router.astype(jnp.float32),
        (((1,), (1,)), ((), ())),
        precision=lax.Precision.HIGHEST,
    )
    grad_in = (cot_wide + jnp.sum(slot_grad.astype(jnp.float32), axis=1) + d_router).astype(
        jnp.bfloat16
    )
    return (
        layer_out,
        grad_in,
        sum_up.astype(jnp.bfloat16)[None],
        sum_down.astype(jnp.bfloat16)[None],
    )


def solution(mesh):
    return jax.shard_map(
        per_device,
        mesh=mesh,
        in_specs=(
            P(("dp", "expert"), None),
            P(("dp", "expert")),
            P(("dp", "expert"), None),
            P(("dp", "expert"), None),
            P(),
            P(),
            P(),
            P(),
            P("expert", None, None),
            P("expert", None, None),
        ),
        out_specs=(
            P(("dp", "expert"), None),
            P(("dp", "expert"), None),
            P("expert", None, None),
            P("expert", None, None),
        ),
        check_vma=False,
    )
```

profile of v0, /device:TPU:1, one launch (start us, length us, event | category | flops | bytes accessed | tf_op | source)
XLA Modules:
  0.0 234.4 jit_solution(15027040676049464937)
XLA Ops:
  13.0 1.4 fusion.22
  15.0 3.5 %scatter_custom_fusion = bf16[1024,512]{1,0:T(8,128)(2,1)} fusion(s32[512]{0:T(512)S(1)} %bitcast.70, bf16[512,512]{1,0:T(8,128)(2,1)S(1)} %reshape.212, bf16[]{:T(256)} %constant.12.clone.1), kind=kCustom, calls=%fused_computation.39 | custom fusion | bytes 1048578 | tf_op jit(solution)/shard_map/scatter | solution.py:86
  18.5 13.3 %all-to-all-start = ((bf16[64,16,512]{2,1,0:T(8,128)(2,1)}), bf16[64,16,512]{2,1,0:T(8,128)(2,1)}, u32[]{:S(2)}, u32[]{:S(2)}) async-start(bf16[64,16,512]{2,1,0:T(8,128)(2,1)} %bitcast.3), calls=%async_computation | async-start | bytes 2097152 | tf_op jit(solution)/shard_map/all_to_all | solution.py:97
  35.7 1.7 mul.134
  37.4 4.3 %scatter_custom_fusion.1 = bf16[1024,512]{1,0:T(8,128)(2,1)} fusion(s32[512]{0:T(512)S(1)} %bitcast.71, f32[512,512]{1,0:T(8,128)} %mul.134, f32[512]{0:T(512)S(1)} %reshape.190, bf16[]{:T(256)} %constant.12.clone.1), kind=kCustom, calls=%fused_computation.35 | custom fusion | flops 524288 | bytes 2099202 | tf_op jit(solution)/shard_map/scatter | solution.py:92
  41.7 18.6 %all-to-all-done = bf16[64,16,512]{2,1,0:T(8,128)(2,1)} async-done(((bf16[64,16,512]{2,1,0:T(8,128)(2,1)}), bf16[64,16,512]{2,1,0:T(8,128)(2,1)}, u32[]{:S(2)}, u32[]{:S(2)}) %all-to-all-start) | async-done | bytes 1048608 | tf_op jit(solution)/shard_map/all_to_all | solution.py:97
  60.3 6.2 %all-to-all-start.2 = ((bf16[64,16,512]{2,1,0:T(8,128)(2,1)}), bf16[64,16,512]{2,1,0:T(8,128)(2,1)S(1)}, u32[]{:S(2)}, u32[]{:S(2)}) async-start(bf16[64,16,512]{2,1,0:T(8,128)(2,1)} %bitcast.9), calls=%async_computation.2 | async-start | bytes 2097152 | tf_op jit(solution)/shard_map/all_to_all | solution.py:103
  66.5 4.3 %fusion.14 = f32[1024,2048]{1,0:T(8,128)S(1)} fusion(bf16[1024,512]{1,0:T(8,128)(2,1)} %bitcast.4, bf16[1,512,2048]{2,1,0:T(8,128)(2,1)} %param.18), kind=kOutput, calls=%fused_computation.23 | convolution fusion | flops 2147483648 | bytes 11534336 | tf_op jit(solution)/shard_map/dot_general | solution.py:34
  70.8 3.2 %copy-done.6 = f32[1024,2048]{1,0:T(8,128)} copy-done((f32[1024,2048]{1,0:T(8,128)}, f32[1024,2048]{1,0:T(8,128)S(1)}, u32[]{:S(2)}) %copy-start.6) | copy-done | bytes 8388632
  74.0 4.0 %fusion.19 = bf16[1024,512]{1,0:T(8,128)(2,1)} fusion(bf16[1,2048,512]{2,1,0:T(8,128)(2,1)S(1)} %copy-done, f32[1024,2048]{1,0:T(8,128)S(1)} %fusion.14), kind=kOutput, calls=%fused_computation.26 | convolution fusion | flops 2166882304 | bytes 11534336 | tf_op jit(solution)/shard_map/dot_general | solution.py:37
  78.0 17.1 %all-to-all-done.2 = bf16[64,16,512]{2,1,0:T(8,128)(2,1)S(1)} async-done(((bf16[64,16,512]{2,1,0:T(8,128)(2,1)}), bf16[64,16,512]{2,1,0:T(8,128)(2,1)S(1)}, u32[]{:S(2)}, u32[]{:S(2)}) %all-to-all-start.2) | async-done | bytes 1048608 | tf_op jit(solution)/shard_map/all_to_all | solution.py:103
  96.0 6.2 %all-to-all-start.1 = ((bf16[64,16,512]{2,1,0:T(8,128)(2,1)}), bf16[64,16,512]{2,1,0:T(8,128)(2,1)S(1)}, u32[]{:S(2)}, u32[]{:S(2)}) async-start(bf16[64,16,512]{2,1,0:T(8,128)(2,1)} %bitcast.65), calls=%async_computation.1 | async-start | bytes 2097152 | tf_op jit(solution)/shard_map/all_to_all | solution.py:100
  102.2 8.8 %fusion.6 = bf16[1024,2048]{1,0:T(8,128)(2,1)S(1)} fusion(f32[1024,2048]{1,0:T(8,128)} %copy-done.6, bf16[1024,512]{1,0:T(8,128)(2,1)} %bitcast.67, bf16[1,2048,512]{2,1,0:T(8,128)(2,1)S(1)} %copy-done), kind=kOutput, calls=%fused_computation.12 | convolution fusion | flops 2187329536 | bytes 15728640 | tf_op jit(solution)/shard_map/dot_general | solution.py:28
  111.0 2.0 copy-done.8
  113.0 5.2 %fusion.7 = bf16[1,512,2048]{2,1,0:T(8,128)(2,1)} fusion(bf16[1024,512]{1,0:T(8,128)(2,1)} %bitcast.4, bf16[1024,2048]{1,0:T(8,128)(2,1)S(1)} %fusion.6), kind=kOutput, calls=%fused_computation.16 | convolution fusion | flops 2148532224 | bytes 7340032 | tf_op jit(solution)/shard_map/dot_general | solution.py:22
  118.2 4.3 %fusion.8 = bf16[1,2048,512]{2,1,0:T(8,128)(2,1)} fusion(bf16[1024,512]{1,0:T(8,128)(2,1)S(1)} %bitcast.68, f32[1024,2048]{1,0:T(8,128)S(1)} %copy-done.7), kind=kOutput, calls=%fused_computation.17 | convolution fusion | flops 2167406592 | bytes 11534336 | tf_op jit(solution)/shard_map/dot_general | solution.py:22
  122.5 6.2 %fusion.16 = bf16[1024,512]{1,0:T(8,128)(2,1)} fusion(bf16[1024,2048]{1,0:T(8,128)(2,1)} %copy-done.8, bf16[1,512,2048]{2,1,0:T(8,128)(2,1)} %param.18), kind=kOutput, calls=%fused_computation.25 | convolution fusion | flops 2148007936 | bytes 7340032 | tf_op jit(solution)/shard_map/dot_general | solution.py:28
  128.7 2.0 all-to-all-done.1
  130.7 8.5 %all-to-all-start.3 = ((bf16[64,16,512]{2,1,0:T(8,128)(2,1)}), bf16[64,16,512]{2,1,0:T(8,128)(2,1)}, u32[]{:S(2)}, u32[]{:S(2)}) async-start(bf16[64,16,512]{2,1,0:T(8,128)(2,1)} %bitcast.66), calls=%async_computation.3 | async-start | bytes 2097152 | tf_op jit(solution)/shard_map/all_to_all | solution.py:108
  139.3 1.8 convert_element_type.80
  141.8 2.6 %gather_fusion = bf16[512,512]{1,0:T(8,128)(2,1)} fusion(bf16[1024,512]{1,0:T(8,128)(2,1)S(1)} %bitcast.64, s32[1024]{0:T(1024)S(1)} %pad_clamp_fusion), kind=kCustom, calls=%fused_computation | custom fusion | bytes 1050624 | tf_op jit(solution)/shard_map/gather | solution.py:111
  144.4 1.7 reshape.188
  146.1 4.0 %multiply_reduce_fusion = (f32[256,2]{1,0:T(8,128)}, f32[256,512]{1,0:T(8,128)}) fusion(f32[256,2,512]{2,1,0:T(2,128)S(1)} %reshape.188, f32[256,512]{1,0:T(8,128)} %convert_element_type.80, f32[256,2]{1,0:T(8,128)S(1)} %copy.28), kind=kLoop, calls=%fused_computation.32 | loop fusion | flops 916992 | bytes 2101248 | tf_op jit(solution)/shard_map/reduce_sum | solution.py:121
  151.1 16.6 %all-to-all-done.3 = bf16[64,16,512]{2,1,0:T(8,128)(2,1)} async-done(((bf16[64,16,512]{2,1,0:T(8,128)(2,1)}), bf16[64,16,512]{2,1,0:T(8,128)(2,1)}, u32[]{:S(2)}, u32[]{:S(2)}) %all-to-all-start.3) | async-done | bytes 1048608 | tf_op jit(solution)/shard_map/all_to_all | solution.py:108
  167.7 4.0 %gather_fusion.1 = bf16[512,512]{1,0:T(8,128)(2,1)} fusion(bf16[1024,512]{1,0:T(8,128)(2,1)} %bitcast.12, s32[1024]{0:T(1024)S(1)} %pad_clamp_fusion), kind=kCustom, calls=%fused_computation.1 | custom fusion | bytes 1050624 | tf_op jit(solution)/shard_map/gather | solution.py:114
  171.7 1.7 reshape.191
  173.4 2.1 reduce_sum.79
  176.3 1.8 add_convert_fusion
  178.1 2.2 fusion.23
  180.4 41.0 %all-reduce.3.cloned.1.call-done = (bf16[1,512,2048]{2,1,0:T(8,128)(2,1)}, bf16[1,2048,512]{2,1,0:T(8,128)(2,1)}) async-done(((bf16[1,512,2048]{2,1,0:T(8,128)(2,1)}, bf16[1,2048,512]{2,1,0:T(8,128)(2,1)}), (bf16[1,512,2048]{2,1,0:T(8,128)(2,1)}, bf16[1,2048,512]{2,1,0:T(8,128)(2,1)})) %all-reduce.3.cloned.1.call-update) | async-done | bytes 4194320 | tf_op jit(solution)/shard_map/psum | solution.py:48
  221.3 3.2 %copy.40 = bf16[1,512,2048]{2,1,0:T(8,128)(2,1)} copy(bf16[1,512,2048]{2,1,0:T(8,128)(2,1)} %get-tuple-element.12) | data formatting | bytes 4194304
  224.5 3.0 %copy.41 = bf16[1,2048,512]{2,1,0:T(8,128)(2,1)} copy(bf16[1,2048,512]{2,1,0:T(8,128)(2,1)} %get-tuple-element.13) | data formatting | bytes 4194304
  (47 shorter events, 13.8 us)
Async XLA Ops:
  7.2 66.8 %copy-start = (bf16[1,2048,512]{2,1,0:T(8,128)(2,1)S(1)}, bf16[1,2048,512]{2,1,0:T(8,128)(2,1)}, u32[]{:S(2)}) copy-start(bf16[1,2048,512]{2,1,0:T(8,128)(2,1)} %param.19) | copy-start | bytes 6291460
  15.0 55.7 %copy-start.5 = (s32[512,1]{0,1:T(1,128)}, s32[512,1]{0,1:T(1,128)S(1)}, u32[]{:S(2)}) copy-start(s32[512,1]{0,1:T(1,128)S(1)} %compare_select_fusion) | copy-start | bytes 6148
  18.5 41.8 %all-to-all-start = ((bf16[64,16,512]{2,1,0:T(8,128)(2,1)}), bf16[64,16,512]{2,1,0:T(8,128)(2,1)}, u32[]{:S(2)}, u32[]{:S(2)}) async-start(bf16[64,16,512]{2,1,0:T(8,128)(2,1)} %bitcast.3), calls=%async_computation | async-start | bytes 2097152 | tf_op jit(solution)/shard_map/all_to_all | solution.py:97
  60.3 34.7 %all-to-all-start.2 = ((bf16[64,16,512]{2,1,0:T(8,128)(2,1)}), bf16[64,16,512]{2,1,0:T(8,128)(2,1)S(1)}, u32[]{:S(2)}, u32[]{:S(2)}) async-start(bf16[64,16,512]{2,1,0:T(8,128)(2,1)} %bitcast.9), calls=%async_computation.2 | async-start | bytes 2097152 | tf_op jit(solution)/shard_map/all_to_all | solution.py:103
  70.8 3.2 %copy-start.6 = (f32[1024,2048]{1,0:T(8,128)}, f32[1024,2048]{1,0:T(8,128)S(1)}, u32[]{:S(2)}) copy-start(f32[1024,2048]{1,0:T(8,128)S(1)} %fusion.14) | copy-start | bytes 25165828
  95.0 1.0 copy-start.1
  96.0 34.7 %all-to-all-start.1 = ((bf16[64,16,512]{2,1,0:T(8,128)(2,1)}), bf16[64,16,512]{2,1,0:T(8,128)(2,1)S(1)}, u32[]{:S(2)}, u32[]{:S(2)}) async-start(bf16[64,16,512]{2,1,0:T(8,128)(2,1)} %bitcast.65), calls=%async_computation.1 | async-start | bytes 2097152 | tf_op jit(solution)/shard_map/all_to_all | solution.py:100
  102.2 119.2 %all-reduce.3.cloned.1.call-start = ((), (), s32[]{:S(2)}) async-start(), calls=%async_computation.4 | async-start | bytes 8388608 | tf_op jit(solution)/shard_map/psum | solution.py:48
  111.0 2.0 copy-start.8
  113.0 5.2 %copy-start.2 = (bf16[64,16,512]{2,1,0:T(8,128)(2,1)S(1)}, bf16[64,16,512]{2,1,0:T(8,128)(2,1)}, u32[]{:S(2)}) copy-start(bf16[64,16,512]{2,1,0:T(8,128)(2,1)} %copy-done.1) | copy-start | bytes 3145732
  113.0 5.2 %copy-start.7 = (f32[1024,2048]{1,0:T(8,128)S(1)}, f32[1024,2048]{1,0:T(8,128)}, u32[]{:S(2)}) copy-start(f32[1024,2048]{1,0:T(8,128)} %copy-done.6) | copy-start | bytes 25165828
  130.7 37.0 %all-to-all-start.3 = ((bf16[64,16,512]{2,1,0:T(8,128)(2,1)}), bf16[64,16,512]{2,1,0:T(8,128)(2,1)}, u32[]{:S(2)}, u32[]{:S(2)}) async-start(bf16[64,16,512]{2,1,0:T(8,128)(2,1)} %bitcast.66), calls=%async_computation.3 | async-start | bytes 2097152 | tf_op jit(solution)/shard_map/all_to_all | solution.py:108
  141.1 35.2 %copy-start.4 = (s32[256,2]{0,1:T(2,128)S(1)}, s32[256,2]{0,1:T(2,128)}, u32[]{:S(2)}) copy-start(s32[256,2]{0,1:T(2,128)} %param.12) | copy-start | bytes 6148
  150.1 28.1 %copy-start.3 = (bf16[512,64]{0,1:T(8,128)(2,1)S(1)}, bf16[512,64]{0,1:T(8,128)(2,1)}, u32[]{:S(2)}) copy-start(bf16[512,64]{0,1:T(8,128)(2,1)} %param.17) | copy-start | bytes 196612
Sparse Core Ops, SparseCore 0:
  122.6 98.6 all-reduce.2
where the time goes:
time: 236 us; the launch traced here: 234 us
  waiting for transfers between devices  95.2 us (40%)
  matrix products  39.4 us (17%)
  starting transfers between devices  34.3 us (15%)
  local copies, waits for them, and re-layouts  32.2 us (14%)
  other arithmetic  19 us (8%)
  between operations  14.2 us (6%)
    psum x1, waiting for transfers between devices, expert_backward(): lax.psum(grad_up_part.astype(jnp.bfloat16), 'dp').astype(jnp.float32)  41 us
    all_to_all x1, waiting for transfers between devices, per_device(): lax.all_to_all(send_in, 'expert', split_axis=0, concat_axis=0, tiled=True)  18.6 us
    all_to_all x1, waiting for transfers between devices, per_device(): lax.all_to_all(send_cot, 'expert', split_axis=0, concat_axis=0, tiled=True)  17.1 us
    all_to_all x1, waiting for transfers between devices, per_device(): lax.all_to_all(d_inputs.reshape(buffer_shape), 'expert', split_axis=0, co...  16.6 us
    dot_general x2, matrix products, contract_cols(): lax.dot_general(left, right, (((1,), (1,)), ((), ())), preferred_element_...  15 us
    all_to_all x1, starting transfers between devices, per_device(): lax.all_to_all(send_in, 'expert', split_axis=0, concat_axis=0, tiled=True)  13.3 us
    unnamed x21, local copies, waits for them, and re-layouts  13.2 us
    dot_general x2, matrix products, contract_rows(): lax.dot_general(left, right, (((0,), (0,)), ((), ())), preferred_element_...  9.5 us
  transfers between devices with their start and end apart: 5, of which 5 were waited for; matrix products, arithmetic and copies ran while one was open for 29% of the time, Pallas kernels for 0%

commit v1 on v0

--- a/solution.py
+++ b/solution.py
@@ -45,7 +45,9 @@
     d_inputs = contract_cols(d_pre, w_up_one).astype(jnp.bfloat16)
     grad_up_part = contract_rows(flat_in, d_pre)
     sum_up, sum_down = (
-        lax.psum(grad_up_part.astype(jnp.bfloat16), "dp").astype(jnp.float32),
+        jnp.sum(lax.all_gather(grad_up_part.astype(jnp.bfloat16), "dp"), axis=0).astype(
+            jnp.float32
+        ),
         lax.psum(grad_down_part.astype(jnp.bfloat16), "dp").astype(jnp.float32),
     )
     return (d_inputs, sum_up, sum_down)

time: 236 us -> 273 us (1.16)
  waiting for transfers between devices: 95.2 us -> 120 us
  matrix products: 39.4 us -> 50.4 us
  other arithmetic: 19 us -> 26.3 us
  local copies, waits for them, and re-layouts: 32.2 us -> 28 us
    all_to_all x1, waiting for transfers between devices: 1.98 us -> 21.9 us  [per_device(): lax.all_to_all(outputs.reshape(buffer_shape), 'expert', split_axis=0, con...]
    psum x1, waiting for transfers between devices: 41 us -> 53.3 us  [expert_backward(): lax.psum(grad_down_part.astype(jnp.bfloat16), 'dp').astype(jnp.float32)]
    all_to_all x1, waiting for transfers between devices: 16.6 us -> 5.37 us  [per_device(): lax.all_to_all(d_inputs.reshape(buffer_shape), 'expert', split_axis=0, co...]
    reduce_sum x0 -> x1, other arithmetic: none -> 7.2 us  [expert_backward(): jnp.sum(lax.all_gather(grad_up_part.astype(jnp.bfloat16), 'dp'), axis=0)]
    unnamed x21 -> x16, local copies, waits for them, and re-layouts: 13.2 us -> 6.76 us
    dot_general x2, matrix products: 9.5 us -> 13.7 us  [contract_rows(): lax.dot_general(left, right, (((0,), (0,)), ((), ())), preferred_element_...]
    all_to_all x1, waiting for transfers between devices: 17.1 us -> 20.8 us  [per_device(): lax.all_to_all(send_cot, 'expert', split_axis=0, concat_axis=0, tiled=True)]
    dot_general x1, matrix products: 4.26 us -> 7.47 us  [expert_forward(): pre_act = jnp.dot(flat_in, w_up_one, preferred_element_type=jnp.float32)]
  transfers between devices with their start and end apart: 5 -> 6, of which waited for: 5 -> 5; matrix products, arithmetic and copies ran while one was open for 29% -> 27% of each run, Pallas kernels for 0% -> 0%
where the time goes in v1:
time: 273 us; the launch traced here: 271 us
  waiting for transfers between devices  120 us (44%)
  matrix products  50.4 us (18%)
  starting transfers between devices  32.4 us (12%)
  local copies, waits for them, and re-layouts  28 us (10%)
  other arithmetic  26.3 us (10%)
  between operations  14.2 us (5%)
    psum x1, waiting for transfers between devices, expert_backward(): lax.psum(grad_down_part.astype(jnp.bfloat16), 'dp').astype(jnp.float32)  53.3 us
    all_to_all x1, waiting for transfers between devices, per_device(): lax.all_to_all(outputs.reshape(buffer_shape), 'expert', split_axis=0, con...  21.9 us
    all_to_all x1, waiting for transfers between devices, per_device(): lax.all_to_all(send_cot, 'expert', split_axis=0, concat_axis=0, tiled=True)  20.8 us
    all_to_all x1, waiting for transfers between devices, per_device(): lax.all_to_all(send_in, 'expert', split_axis=0, concat_axis=0, tiled=True)  18.6 us
    dot_general x2, matrix products, contract_cols(): lax.dot_general(left, right, (((1,), (1,)), ((), ())), preferred_element_...  15.3 us
    dot_general x2, matrix products, contract_rows(): lax.dot_general(left, right, (((0,), (0,)), ((), ())), preferred_element_...  13.7 us
    all_to_all x1, starting transfers between devices, per_device(): lax.all_to_all(send_in, 'expert', split_axis=0, concat_axis=0, tiled=True)  13.3 us
    dot_general x1, matrix products, expert_forward(): pre_act = jnp.dot(flat_in, w_up_one, preferred_element_type=jnp.float32)  7.47 us
  transfers between devices with their start and end apart: 6, of which 5 were waited for; matrix products, arithmetic and copies ran while one was open for 27% of the time, Pallas kernels for 0%

profile of v1, /device:TPU:1, one launch (start us, length us, event | category | flops | bytes accessed | tf_op | source)
XLA Modules:
  0.0 271.3 jit_solution(18171868954820905938)
XLA Ops:
  13.0 1.4 fusion.21
  15.8 4.0 %scatter_custom_fusion = bf16[1024,512]{1,0:T(8,128)(2,1)} fusion(s32[512]{0:T(512)S(1)} %bitcast.73, bf16[512,512]{1,0:T(8,128)(2,1)} %reshape.212, bf16[]{:T(256)} %constant.12.clone.1), kind=kCustom, calls=%fused_computation.38 | custom fusion | bytes 1049088 | tf_op jit(solution)/shard_map/scatter | solution.py:88
  19.8 13.3 %all-to-all-start = ((bf16[64,16,512]{2,1,0:T(8,128)(2,1)}), bf16[64,16,512]{2,1,0:T(8,128)(2,1)}, u32[]{:S(2)}, u32[]{:S(2)}) async-start(bf16[64,16,512]{2,1,0:T(8,128)(2,1)} %bitcast.3), calls=%async_computation | async-start | bytes 2097152 | tf_op jit(solution)/shard_map/all_to_all | solution.py:99
  35.8 1.2 mul.133
  37.0 1.7 mul.134
  38.7 4.2 %scatter_custom_fusion.1 = bf16[1024,512]{1,0:T(8,128)(2,1)} fusion(s32[512]{0:T(512)S(1)} %bitcast.74, f32[512,512]{1,0:T(8,128)} %mul.134, f32[512]{0:T(512)S(1)} %reshape.190, bf16[]{:T(256)} %constant.12.clone.1), kind=kCustom, calls=%fused_computation.34 | custom fusion | flops 524288 | bytes 2099202 | tf_op jit(solution)/shard_map/scatter | solution.py:94
  42.9 18.6 %all-to-all-done = bf16[64,16,512]{2,1,0:T(8,128)(2,1)} async-done(((bf16[64,16,512]{2,1,0:T(8,128)(2,1)}), bf16[64,16,512]{2,1,0:T(8,128)(2,1)}, u32[]{:S(2)}, u32[]{:S(2)}) %all-to-all-start) | async-done | bytes 1048608 | tf_op jit(solution)/shard_map/all_to_all | solution.py:99
  61.6 6.2 %all-to-all-start.2 = ((bf16[64,16,512]{2,1,0:T(8,128)(2,1)}), bf16[64,16,512]{2,1,0:T(8,128)(2,1)S(1)}, u32[]{:S(2)}, u32[]{:S(2)}) async-start(bf16[64,16,512]{2,1,0:T(8,128)(2,1)} %bitcast.9), calls=%async_computation.2 | async-start | bytes 2097152 | tf_op jit(solution)/shard_map/all_to_all | solution.py:105
  68.0 7.5 %fusion.13 = f32[1024,2048]{1,0:T(8,128)} fusion(bf16[1024,512]{1,0:T(8,128)(2,1)} %bitcast.4, bf16[1,512,2048]{2,1,0:T(8,128)(2,1)} %param.18), kind=kOutput, calls=%fused_computation.22 | convolution fusion | flops 2147483648 | bytes 11534336 | tf_op jit(solution)/shard_map/dot_general | solution.py:34
  75.5 20.8 %all-to-all-done.2 = bf16[64,16,512]{2,1,0:T(8,128)(2,1)S(1)} async-done(((bf16[64,16,512]{2,1,0:T(8,128)(2,1)}), bf16[64,16,512]{2,1,0:T(8,128)(2,1)S(1)}, u32[]{:S(2)}, u32[]{:S(2)}) %all-to-all-start.2) | async-done | bytes 1048608 | tf_op jit(solution)/shard_map/all_to_all | solution.py:105
  96.3 8.6 %fusion.6 = bf16[1024,2048]{1,0:T(8,128)(2,1)S(1)} fusion(f32[1024,2048]{1,0:T(8,128)} %fusion.13, bf16[1024,512]{1,0:T(8,128)(2,1)S(1)} %bitcast.68, bf16[1,2048,512]{2,1,0:T(8,128)(2,1)S(1)} %copy-done), kind=kOutput, calls=%fused_computation.12 | convolution fusion | flops 2187329536 | bytes 15728640 | tf_op jit(solution)/shard_map/dot_general | solution.py:28
  105.0 1.9 copy-done.6
  106.9 5.0 %convolution_convert_fusion.1 = bf16[512,2048]{1,0:T(8,128)(2,1)} fusion(bf16[1024,512]{1,0:T(8,128)(2,1)} %bitcast.4, bf16[1024,2048]{1,0:T(8,128)(2,1)S(1)} %fusion.6), kind=kOutput, calls=%fused_computation.15 | convolution fusion | flops 2148532224 | bytes 7340032 | tf_op jit(solution)/shard_map/dot_general | solution.py:22
  111.9 7.1 %fusion.18 = bf16[1024,512]{1,0:T(8,128)(2,1)} fusion(bf16[1,2048,512]{2,1,0:T(8,128)(2,1)S(1)} %copy-done, f32[1024,2048]{1,0:T(8,128)} %fusion.13), kind=kOutput, calls=%fused_computation.25 | convolution fusion | flops 2166882304 | bytes 11534336 | tf_op jit(solution)/shard_map/dot_general | solution.py:37
  119.0 6.2 %all-to-all-start.1 = ((bf16[64,16,512]{2,1,0:T(8,128)(2,1)}), bf16[64,16,512]{2,1,0:T(8,128)(2,1)S(1)}, u32[]{:S(2)}, u32[]{:S(2)}) async-start(bf16[64,16,512]{2,1,0:T(8,128)(2,1)} %bitcast.71), calls=%async_computation.1 | async-start | bytes 2097152 | tf_op jit(solution)/shard_map/all_to_all | solution.py:102
  125.2 6.7 %fusion.15 = bf16[1024,512]{1,0:T(8,128)(2,1)} fusion(bf16[1024,2048]{1,0:T(8,128)(2,1)} %copy-done.6, bf16[1,512,2048]{2,1,0:T(8,128)(2,1)} %param.18), kind=kOutput, calls=%fused_computation.24 | convolution fusion | flops 2148007936 | bytes 7340032 | tf_op jit(solution)/shard_map/dot_general | solution.py:28
  131.9 21.9 %all-to-all-done.1 = bf16[64,16,512]{2,1,0:T(8,128)(2,1)S(1)} async-done(((bf16[64,16,512]{2,1,0:T(8,128)(2,1)}), bf16[64,16,512]{2,1,0:T(8,128)(2,1)S(1)}, u32[]{:S(2)}, u32[]{:S(2)}) %all-to-all-start.1) | async-done | bytes 1048608 | tf_op jit(solution)/shard_map/all_to_all | solution.py:102
  154.7 6.4 %all-to-all-start.3 = ((bf16[64,16,512]{2,1,0:T(8,128)(2,1)}), bf16[64,16,512]{2,1,0:T(8,128)(2,1)S(1)}, u32[]{:S(2)}, u32[]{:S(2)}) async-start(bf16[64,16,512]{2,1,0:T(8,128)(2,1)} %bitcast.70), calls=%async_computation.3 | async-start | bytes 2097152 | tf_op jit(solution)/shard_map/all_to_all | solution.py:110
  161.2 8.7 %fusion.7 = bf16[1,2048,512]{2,1,0:T(8,128)(2,1)} fusion(bf16[1024,512]{1,0:T(8,128)(2,1)} %bitcast.69, f32[1024,2048]{1,0:T(8,128)} %fusion.13), kind=kOutput, calls=%fused_computation.16 | convolution fusion | flops 2167406592 | bytes 11534336 | tf_op jit(solution)/shard_map/dot_general | solution.py:22
  169.9 1.8 convert_element_type.82
  172.4 4.0 %gather_fusion = bf16[512,512]{1,0:T(8,128)(2,1)} fusion(bf16[1024,512]{1,0:T(8,128)(2,1)} %bitcast.65, s32[1024]{0:T(1024)S(1)} %pad_clamp_fusion), kind=kCustom, calls=%fused_computation | custom fusion | bytes 1050624 | tf_op jit(solution)/shard_map/gather | solution.py:113
  176.5 2.7 reshape.188
  179.1 4.1 %multiply_reduce_fusion = (f32[256,2]{1,0:T(8,128)}, f32[256,512]{1,0:T(8,128)}) fusion(f32[256,2,512]{2,1,0:T(2,128)} %reshape.188, f32[256,512]{1,0:T(8,128)} %convert_element_type.82, f32[256,2]{1,0:T(8,128)S(1)} %copy.28), kind=kLoop, calls=%fused_computation.31 | loop fusion | flops 916992 | bytes 2101248 | tf_op jit(solution)/shard_map/reduce_sum | solution.py:123
  184.3 5.4 %all-to-all-done.3 = bf16[64,16,512]{2,1,0:T(8,128)(2,1)S(1)} async-done(((bf16[64,16,512]{2,1,0:T(8,128)(2,1)}), bf16[64,16,512]{2,1,0:T(8,128)(2,1)S(1)}, u32[]{:S(2)}, u32[]{:S(2)}) %all-to-all-start.3) | async-done | bytes 1048608 | tf_op jit(solution)/shard_map/all_to_all | solution.py:110
  189.7 2.6 gather_fusion.1
  192.3 1.7 reshape.191
  194.0 2.1 reduce_sum.91
  196.9 1.8 add_convert_fusion
  198.7 2.2 fusion.22
  200.9 7.2 %reduce_sum.95 = bf16[512,2048]{1,0:T(8,128)(2,1)} reduce(bf16[4,512,2048]{2,1,0:T(8,128)(2,1)} %bitcast.66, bf16[]{:T(256)} %constant.12.clone.1), dimensions={0}, to_apply=%region_12.13 | reduce | flops 3145728 | bytes 10485762 | tf_op jit(solution)/shard_map/reduce_sum | solution.py:48
  208.1 53.3 %all-reduce.2.cloned.1.call-done = bf16[1,2048,512]{2,1,0:T(8,128)(2,1)} async-done(((bf16[1,2048,512]{2,1,0:T(8,128)(2,1)}), bf16[1,2048,512]{2,1,0:T(8,128)(2,1)}) %all-reduce.2.cloned.1.call-update) | async-done | bytes 2097168 | tf_op jit(solution)/shard_map/psum | solution.py:51
  261.4 3.0 %copy.39 = bf16[1,2048,512]{2,1,0:T(8,128)(2,1)} copy(bf16[1,2048,512]{2,1,0:T(8,128)(2,1)} %all-reduce.2.cloned.1.call-done) | data formatting | bytes 4194304
  (46 shorter events, 13.6 us)
Async XLA Ops:
  7.2 89.1 %copy-start = (bf16[1,2048,512]{2,1,0:T(8,128)(2,1)S(1)}, bf16[1,2048,512]{2,1,0:T(8,128)(2,1)}, u32[]{:S(2)}) copy-start(bf16[1,2048,512]{2,1,0:T(8,128)(2,1)} %param.19) | copy-start | bytes 6291460
  15.8 59.7 %copy-start.5 = (s32[512,1]{0,1:T(1,128)}, s32[512,1]{0,1:T(1,128)S(1)}, u32[]{:S(2)}) copy-start(s32[512,1]{0,1:T(1,128)S(1)} %compare_select_fusion) | copy-start | bytes 6148
  19.8 41.8 %all-to-all-start = ((bf16[64,16,512]{2,1,0:T(8,128)(2,1)}), bf16[64,16,512]{2,1,0:T(8,128)(2,1)}, u32[]{:S(2)}, u32[]{:S(2)}) async-start(bf16[64,16,512]{2,1,0:T(8,128)(2,1)} %bitcast.3), calls=%async_computation | async-start | bytes 2097152 | tf_op jit(solution)/shard_map/all_to_all | solution.py:99
  61.6 34.7 %all-to-all-start.2 = ((bf16[64,16,512]{2,1,0:T(8,128)(2,1)}), bf16[64,16,512]{2,1,0:T(8,128)(2,1)S(1)}, u32[]{:S(2)}, u32[]{:S(2)}) async-start(bf16[64,16,512]{2,1,0:T(8,128)(2,1)} %bitcast.9), calls=%async_computation.2 | async-start | bytes 2097152 | tf_op jit(solution)/shard_map/all_to_all | solution.py:105
  67.8 133.2 %all-gather.3.cloned.1.call-start = ((), (), s32[]{:S(2)}) async-start(), calls=%async_computation.5 | async-start | bytes 10485760 | tf_op jit(solution)/shard_map/all_gather | solution.py:48
  96.3 8.7 %copy-start.2 = (bf16[64,16,512]{2,1,0:T(8,128)(2,1)}, bf16[64,16,512]{2,1,0:T(8,128)(2,1)S(1)}, u32[]{:S(2)}) copy-start(bf16[64,16,512]{2,1,0:T(8,128)(2,1)S(1)} %all-to-all-done.2) | copy-start | bytes 3145732
  104.9 1.9 copy-start.6
  119.0 34.7 %all-to-all-start.1 = ((bf16[64,16,512]{2,1,0:T(8,128)(2,1)}), bf16[64,16,512]{2,1,0:T(8,128)(2,1)S(1)}, u32[]{:S(2)}, u32[]{:S(2)}) async-start(bf16[64,16,512]{2,1,0:T(8,128)(2,1)} %bitcast.71), calls=%async_computation.1 | async-start | bytes 2097152 | tf_op jit(solution)/shard_map/all_to_all | solution.py:102
  153.7 1.0 copy-start.1
  154.7 35.0 %all-to-all-start.3 = ((bf16[64,16,512]{2,1,0:T(8,128)(2,1)}), bf16[64,16,512]{2,1,0:T(8,128)(2,1)S(1)}, u32[]{:S(2)}, u32[]{:S(2)}) async-start(bf16[64,16,512]{2,1,0:T(8,128)(2,1)} %bitcast.70), calls=%async_computation.3 | async-start | bytes 2097152 | tf_op jit(solution)/shard_map/all_to_all | solution.py:110
  161.1 100.3 %all-reduce.2.cloned.1.call-start = ((), (), s32[]{:S(2)}) async-start(), calls=%async_computation.4 | async-start | bytes 4194304 | tf_op jit(solution)/shard_map/psum | solution.py:51
  171.7 25.1 %copy-start.4 = (s32[256,2]{0,1:T(2,128)S(1)}, s32[256,2]{0,1:T(2,128)}, u32[]{:S(2)}) copy-start(s32[256,2]{0,1:T(2,128)} %param.12) | copy-start | bytes 6148
  183.3 15.4 %copy-start.3 = (bf16[512,64]{0,1:T(8,128)(2,1)S(1)}, bf16[512,64]{0,1:T(8,128)(2,1)}, u32[]{:S(2)}) copy-start(bf16[512,64]{0,1:T(8,128)(2,1)} %param.17) | copy-start | bytes 196612
Sparse Core Ops, SparseCore 0:
  112.0 82.2 all-gather.2
  196.7 64.7 all-reduce.1
